TPU v7x, 32 devices: a whole 2x2x4 slice. The times are simulated.
32 devices in a mesh: tile: 8 (over z, core), deg: 4 (over y, x).
Axes of the slice: x: 2, y: 2, z: 4, core: 2. Of those that a mesh axis runs over, the one named last changes fastest.
Arguments:
- field: float32 [3, 8, 128, 512], P(None, None, 'tile', 'deg'), may hold values from -6 to 6
- flow: float32 [3, 8, 128, 512], P(None, None, 'tile', 'deg'), may hold values from -3 to 3
- match_ops: bfloat16 [32, 512, 512], P(('tile', 'deg')), may hold values from -0.5 to 20.5
- wave_of_slot: int32 [32], replicated, may hold values from 0 to 31, each once
Outputs:
- advanced: float32 [3, 8, 128, 512], P(None, None, 'tile', 'deg')
Inputs may be any that keep to these rules, and one draw needn't show every extreme that they name: `wave_of_slot`: every wavenumber from 0 to 31 is named by exactly one slot.
All inputs are finite; a program needn't handle non-finite values.
Results may differ from a plain program's by a relative error of at most 0.00065.
Values may be sent and summed in bfloat16 or wider, within the bound.
No kernel may reach another device: no remote copies, remote signals or barrier semaphores. Data moves between devices by JAX's collectives and lax.ppermute only.
A program may use at most 64 MiB of HBM per device.

v0:
```python
import math
import jax
import jax.numpy as jnp
from jax import lax
from jax.sharding import PartitionSpec as P

P_SIZE = 8
diffusivity = 0.05
time_step = 0.01
highest = lax.Precision.HIGHEST
gll_interior = [0.2092992179024789, 0.5917001814331423, 0.8717401485096066]


def padded_2(value, sides, width):
    for axis, dim in sides:
        size, length = (lax.axis_size(axis), value.shape[dim])
        up = [(i, (i + 1) % size) for i in range(size)]
        down = [(j, i) for i, j in up]
        last = lax.slice_in_dim(value, length - width, length, axis=dim)
        first = lax.slice_in_dim(value, 0, width, axis=dim)
        before = lax.ppermute(last, axis, up)
        after = lax.ppermute(first, axis, down)
        value = jnp.concatenate([before, value, after], axis=dim)
    return value


def legendre_value(point, degree):
    previous = 1.0
    current = point
    for order in range(1, degree):
        following = ((2 * order + 1) * point * current - order * previous) / (order + 1)
        previous = current
        current = following
    return current


def gll_tables(count):
    degree = count - 1
    points = [-1.0] + [-value for value in reversed(gll_interior)] + list(gll_interior) + [1.0]
    values = [legendre_value(point, degree) for point in points]
    weights = [2.0 / (degree * (degree + 1) * value * value) for value in values]
    matrix = [
        [
            values[row] / (values[col] * (points[row] - points[col])) if row != col else 0.0
            for col in range(count)
        ]
        for row in range(count)
    ]
    matrix[0][0] = -degree * (degree + 1) / 4.0
    matrix[count - 1][count - 1] = degree * (degree + 1) / 4.0
    return (points, weights, matrix)


def apply_along(values, axis_pos, matrix):
    shape = values.shape
    blocks = values.reshape(
        shape[:axis_pos] + (shape[axis_pos] // P_SIZE, P_SIZE) + shape[axis_pos + 1 :]
    )
    letters = list("abcdefg"[: blocks.ndim])
    source = list(letters)
    source[axis_pos + 1] = "p"
    target = list(letters)
    target[axis_pos + 1] = "q"
    formula = "".join(source) + ",qp->" + "".join(target)
    return jnp.einsum(formula, blocks, matrix, precision=highest).reshape(shape)


def assemble_dim(values, axis_pos, left, right):
    shape = values.shape
    count = shape[axis_pos] // P_SIZE
    blocks = values.reshape(shape[:axis_pos] + (count, P_SIZE) + shape[axis_pos + 1 :])
    edge_shape = shape[:axis_pos] + (1, 1) + shape[axis_pos + 1 :]
    first = lax.slice_in_dim(blocks, 0, 1, axis=axis_pos + 1)
    last = lax.slice_in_dim(blocks, P_SIZE - 1, P_SIZE, axis=axis_pos + 1)
    before = jnp.concatenate(
        [left.reshape(edge_shape), lax.slice_in_dim(last, 0, count - 1, axis=axis_pos)],
        axis=axis_pos,
    )
    after = jnp.concatenate(
        [lax.slice_in_dim(first, 1, count, axis=axis_pos), right.reshape(edge_shape)], axis=axis_pos
    )
    middle = lax.slice_in_dim(blocks, 1, P_SIZE - 1, axis=axis_pos + 1)
    joined = jnp.concatenate([first + before, middle, last + after], axis=axis_pos + 1)
    return joined.reshape(shape)


def assembled_weights(weights, count, lead, trail):
    position = jnp.arange(count * P_SIZE, dtype=jnp.int32)
    local_point = position % P_SIZE
    element = position // P_SIZE
    base = jnp.tile(weights, count)
    starts = (
        jnp.where(local_point == 0, jnp.where(element > 0, 1.0, lead), 0.0) * weights[P_SIZE - 1]
    )
    ends = (
        jnp.where(local_point == P_SIZE - 1, jnp.where(element < count - 1, 1.0, trail), 0.0)
        * weights[0]
    )
    return base + starts + ends


def phases(waves, elem_start, elem_count, span, points):
    element = elem_start + jnp.arange(elem_count * P_SIZE, dtype=jnp.int32) // P_SIZE
    whole = waves[:, None] * (2 * element + 1)[None, :] % span
    fraction = waves.astype(jnp.float32)[:, None] * jnp.tile(points, elem_count)[None, :]
    return 2.0 * math.pi / span * (whole.astype(jnp.float32) + fraction)


def local(field, flow, match_ops, wave_of_slot):
    tiles = lax.axis_size("tile")
    groups = lax.axis_size("deg")
    tile_index = lax.axis_index("tile")
    group_index = lax.axis_index("deg")
    radial_nodes = field.shape[1]
    na_dev = field.shape[2]
    nb_dev = field.shape[3]
    elems_a = na_dev // P_SIZE
    elems_b = nb_dev // P_SIZE
    span = 2 * elems_a * tiles
    per_tile = wave_of_slot.shape[0] // tiles
    scale = P_SIZE / (na_dev * tiles)
    points_list, weights_list, matrix_list = gll_tables(P_SIZE)
    points = jnp.asarray(points_list, jnp.float32)
    weights = jnp.asarray(weights_list, jnp.float32)
    dmat = jnp.asarray(matrix_list, jnp.float32)
    block = jnp.kron(jnp.eye(elems_b, dtype=jnp.float32), dmat)
    lead = (group_index > 0).astype(jnp.float32)
    trail = (group_index < groups - 1).astype(jnp.float32)
    w_r = jnp.tile(weights, radial_nodes // P_SIZE)
    w_a = jnp.tile(weights, elems_a)
    w_b = jnp.tile(weights, elems_b)
    mass3 = w_r[:, None, None] * w_a[None, :, None] * w_b[None, None, :]
    surface_weight = w_a[:, None] * w_b[None, :]
    assembled = (
        assembled_weights(weights, radial_nodes // P_SIZE, 0.0, 0.0)[:, None, None]
        * assembled_weights(weights, elems_a, 1.0, 1.0)[None, :, None]
        * assembled_weights(weights, elems_b, lead, trail)[None, None, :]
    )
    column_mask = jnp.concatenate([lead[None], jnp.ones((nb_dev,), jnp.float32), trail[None]])

    def derive(values, direction, transpose):
        if direction == 2:
            table = block if transpose else block.T
            return jnp.dot(values, table, precision=highest)
        return apply_along(values, direction, dmat.T if transpose else dmat)

    flow_parts = [flow[0], flow[1], flow[2]]
    grad_flow = [
        [derive(flow_parts[component], direction, False) for direction in range(3)]
        for component in range(3)
    ]

    def analyse(surface):
        angle = phases(wave_of_slot, tile_index * elems_a, elems_a, span, points)
        table = (
            jnp.stack([jnp.cos(angle), jnp.sin(angle)], axis=1) * (w_a * scale)[None, None, :]
        ).reshape(lax.axis_size("tile") * per_tile * 2, na_dev)
        return jnp.dot(table, surface, precision=highest).reshape(
            lax.axis_size("tile") * per_tile, 2, nb_dev
        )

    def surface_flux(surface):
        coeff = lax.psum_scatter(analyse(surface), "tile", scatter_dimension=0, tiled=True)
        owned = lax.all_to_all(
            coeff.astype(jnp.bfloat16), "deg", split_axis=0, concat_axis=2, tiled=True
        )
        mapped = jnp.einsum("kpq,kcq->kcp", match_ops, owned, preferred_element_type=jnp.float32)
        matched = lax.all_to_all(mapped, "deg", split_axis=2, concat_axis=0, tiled=True)
        my_waves = lax.dynamic_slice_in_dim(wave_of_slot, tile_index * per_tile, per_tile)
        flat_matched = matched.reshape(per_tile * 2, nb_dev)
        angle = phases(
            my_waves, jnp.int32(0) // P_SIZE, lax.axis_size("tile") * na_dev // P_SIZE, span, points
        )
        table = jnp.stack([jnp.cos(angle).T, jnp.sin(angle).T], axis=2).reshape(
            lax.axis_size("tile") * na_dev, per_tile * 2
        )
        total = lax.psum_scatter(
            jnp.dot(table, flat_matched, precision=highest), "tile", scatter_dimension=0, tiled=True
        )
        return -total

    def tendency(parts):
        rhs = []
        for component in range(3):
            slopes = [derive(parts[component], direction, False) for direction in range(3)]
            stretch = (
                parts[0] * grad_flow[component][0]
                + parts[1] * grad_flow[component][1]
                + parts[2] * grad_flow[component][2]
            )
            carried = (
                flow_parts[0] * slopes[0] + flow_parts[1] * slopes[1] + flow_parts[2] * slopes[2]
            )
            spread = (
                derive(mass3 * slopes[0], 0, True)
                + derive(mass3 * slopes[1], 1, True)
                + derive(mass3 * slopes[2], 2, True)
            )
            rhs.append(mass3 * (stretch - carried) - diffusivity * spread)
        flux = surface_flux(parts[0][radial_nodes - 1])
        rhs[0] = rhs[0].at[radial_nodes - 1].add(diffusivity * surface_weight * flux)
        stacked = jnp.stack(rhs)
        plane_r = jnp.zeros_like(lax.slice_in_dim(stacked, 0, 1, axis=1))
        stacked = assemble_dim(stacked, 1, plane_r, plane_r)
        padded = padded_2(stacked.astype(jnp.bfloat16), (("tile", 2), ("deg", 3)), 1).astype(
            stacked.dtype
        )
        padded = padded * column_mask
        along_a = assemble_dim(padded[:, :, 1:-1, :], 2, padded[:, :, 0:1, :], padded[:, :, -1:, :])
        along_b = assemble_dim(
            along_a[:, :, :, 1:-1], 3, along_a[:, :, :, 0:1], along_a[:, :, :, -1:]
        )
        return along_b / assembled[None]

    section = field + time_step * tendency([field[0], field[1], field[2]])
    return 0.5 * (field + section + time_step * tendency([section[0], section[1], section[2]]))


def solution(mesh):
    placed = (
        P(None, None, "tile", "deg"),
        P(None, None, "tile", "deg"),
        P(("tile", "deg"), None, None),
        P(),
    )
    return jax.shard_map(
        local, mesh=mesh, in_specs=placed, out_specs=P(None, None, "tile", "deg"), check_vma=False
    )
```

profile of v0, /device:TPU:0, one launch (start us, length us, event | category | flops | bytes accessed | tf_op | source)
XLA Modules:
  0.0 227.2 jit_solution(8538211180107501560)
XLA Ops:
  6.5 0.7 tile.8
  7.3 0.7 tile.11
  8.1 0.7 convert_element_type.71
  8.8 0.8 fusion.130
  10.2 1.0 fusion.116
  11.2 30.3 %all-reduce = bf16[32,2,128]{2,0,1:T(8,128)(2,1)S(1)} all-reduce(f32[32,2,128]{2,0,1:T(8,128)S(1)} %fusion.116), channel_id=2, replica_groups=mesh['tile'=8,'deg'=4] {'tile'}, use_global_device_ids=true, to_apply=%region_0.1.clone | all-reduce | flops 8192 | bytes 49152
  41.5 1.2 dynamic-slice.16
  43.9 3.7 %all-to-all-start = ((bf16[4,2,128]{2,1,0:T(2,128)(2,1)}), bf16[4,2,128]{2,1,0:T(2,128)(2,1)S(1)}, u32[]{:S(2)}, u32[]{:S(2)}) async-start(bf16[4,2,128]{2,1,0:T(2,128)(2,1)} %copy.334), calls=%async_computation | async-start | bytes 4096 | tf_op jit(solution)/shard_map/all_to_all | solution.py:164
  47.7 0.8 broadcast_multiply_fusion.3
  48.5 0.9 slice_bitcast_fusion.6
  49.4 1.1 fusion.51
  50.5 1.0 convolution_bitcast_fusion.6
  51.6 0.9 fusion.169
  52.6 0.7 broadcast_multiply_fusion.5
  53.3 1.0 fusion.54
  54.4 0.8 broadcast_multiply_fusion
  62.6 1.2 reduce.4
  63.8 0.8 reshape.1012
  64.6 4.2 %all-to-all-start.1 = ((f32[4,1,256]{2,1,0:T(1,128)}), f32[4,1,256]{2,1,0:T(1,128)S(1)}, u32[]{:S(2)}, u32[]{:S(2)}) async-start(f32[4,1,256]{2,1,0:T(1,128)} %reshape.1012), calls=%async_computation.1 | async-start | bytes 8192 | tf_op jit(solution)/shard_map/all_to_all | solution.py:168
  68.8 4.7 %all-to-all-done.1 = f32[4,1,256]{2,1,0:T(1,128)S(1)} async-done(((f32[4,1,256]{2,1,0:T(1,128)}), f32[4,1,256]{2,1,0:T(1,128)S(1)}, u32[]{:S(2)}, u32[]{:S(2)}) %all-to-all-start.1) | async-done | bytes 4128 | tf_op jit(solution)/shard_map/all_to_all | solution.py:168
  74.6 0.9 fusion.172
  76.1 25.9 %reduce-scatter.5.cloned.1.call-done = f32[16,128]{1,0:T(8,128)} async-done(((f32[128,128]{1,0:T(8,128)}), f32[16,128]{1,0:T(8,128)}) %reduce-scatter.5.cloned.1.call-update) | async-done | bytes 8208 | tf_op jit(solution)/shard_map/reduce_scatter | solution.py:177
  102.0 0.8 fusion.123
  103.5 0.9 collective-permute-done.1
  104.4 3.5 %collective-permute-done = bf16[3,8,1,128]{3,1,2,0:T(8,128)(2,1)S(1)} collective-permute-done((bf16[3,8,1,128]{3,1,2,0:T(8,128)(2,1)S(1)}, bf16[3,8,1,128]{3,1,2,0:T(8,128)(2,1)S(1)}, u32[]{:S(2)}, u32[]{:S(2)}) %collective-permute-start) | collective-permute-done | bytes 6176 | tf_op jit(solution)/shard_map/ppermute | solution.py:21
  108.0 2.7 %collective-permute-start.3 = (bf16[3,8,18,1]{3,1,2,0:T(8,128)(2,1)S(1)}, bf16[3,8,18,1]{3,1,2,0:T(8,128)(2,1)S(1)}, u32[]{:S(2)}, u32[]{:S(2)}) collective-permute-start(bf16[3,8,18,1]{3,1,2,0:T(8,128)(2,1)S(1)} %get-tuple-element.73), channel_id=1, source_target_pairs={{1,0},{2,1},{3,2},{0,3},{5,4},{6,5},{7,6},{4,7},{9,8},{10,9},{11,1... | collective-permute-start | bytes 2600 | tf_op jit(solution)/shard_map/ppermute | solution.py:22
  110.8 2.2 collective-permute-done.3
  113.0 3.3 %collective-permute-done.2 = bf16[3,8,18,1]{3,1,2,0:T(8,128)(2,1)S(1)} collective-permute-done((bf16[3,8,18,1]{3,1,2,0:T(8,128)(2,1)S(1)}, bf16[3,8,18,1]{3,1,2,0:T(8,128)(2,1)S(1)}, u32[]{:S(2)}, u32[]{:S(2)}) %collective-permute-start.2) | collective-permute-done | bytes 896 | tf_op jit(solution)/shard_map/ppermute | solution.py:21
  117.7 1.3 slice.297
  120.0 2.0 maximum_bitcast_fusion
  126.1 26.0 %all-reduce.1 = bf16[32,2,128]{2,0,1:T(8,128)(2,1)S(1)} all-reduce(f32[32,2,128]{2,0,1:T(8,128)S(1)} %fusion.115), channel_id=4, replica_groups=mesh['tile'=8,'deg'=4] {'tile'}, use_global_device_ids=true, to_apply=%region_2.3.clone | all-reduce | flops 8192 | bytes 49152
  152.7 3.2 %all-to-all-start.2 = ((bf16[4,2,128]{2,1,0:T(2,128)(2,1)}), bf16[4,2,128]{2,1,0:T(2,128)(2,1)S(1)}, u32[]{:S(2)}, u32[]{:S(2)}) async-start(bf16[4,2,128]{2,1,0:T(2,128)(2,1)} %copy.387), calls=%async_computation.3 | async-start | bytes 4096 | tf_op jit(solution)/shard_map/all_to_all | solution.py:164
  156.9 3.5 %all-to-all-done.2 = bf16[4,2,128]{2,1,0:T(2,128)(2,1)S(1)} async-done(((bf16[4,2,128]{2,1,0:T(2,128)(2,1)}), bf16[4,2,128]{2,1,0:T(2,128)(2,1)S(1)}, u32[]{:S(2)}, u32[]{:S(2)}) %all-to-all-start.2) | async-done | bytes 2080 | tf_op jit(solution)/shard_map/all_to_all | solution.py:164
  160.7 1.2 reduce.6
  161.9 0.8 reshape.1014
  162.7 3.2 %all-to-all-start.3 = ((f32[4,1,256]{2,1,0:T(1,128)}), f32[4,1,256]{2,1,0:T(1,128)S(1)}, u32[]{:S(2)}, u32[]{:S(2)}) async-start(f32[4,1,256]{2,1,0:T(1,128)} %reshape.1014), calls=%async_computation.4 | async-start | bytes 8192 | tf_op jit(solution)/shard_map/all_to_all | solution.py:168
  166.3 4.3 %all-to-all-done.3 = f32[4,1,256]{2,1,0:T(1,128)S(1)} async-done(((f32[4,1,256]{2,1,0:T(1,128)}), f32[4,1,256]{2,1,0:T(1,128)S(1)}, u32[]{:S(2)}, u32[]{:S(2)}) %all-to-all-start.3) | async-done | bytes 4128 | tf_op jit(solution)/shard_map/all_to_all | solution.py:168
  171.7 0.9 fusion.173
  172.9 26.3 %reduce-scatter.7.cloned.1.call-done = f32[16,128]{1,0:T(8,128)} async-done(((f32[128,128]{1,0:T(8,128)}), f32[16,128]{1,0:T(8,128)}) %reduce-scatter.7.cloned.1.call-update) | async-done | bytes 8208 | tf_op jit(solution)/shard_map/reduce_scatter | solution.py:177
  199.2 0.8 negate_multiply_fusion
  200.6 0.9 collective-permute-done.5
  201.6 3.5 %collective-permute-done.4 = bf16[3,8,1,128]{3,1,2,0:T(8,128)(2,1)S(1)} collective-permute-done((bf16[3,8,1,128]{3,1,2,0:T(8,128)(2,1)S(1)}, bf16[3,8,1,128]{3,1,2,0:T(8,128)(2,1)S(1)}, u32[]{:S(2)}, u32[]{:S(2)}) %collective-permute-start.4) | collective-permute-done | bytes 6176 | tf_op jit(solution)/shard_map/ppermute | solution.py:21
  205.2 2.7 %collective-permute-start.7 = (bf16[3,8,18,1]{3,1,2,0:T(8,128)(2,1)S(1)}, bf16[3,8,18,1]{3,1,2,0:T(8,128)(2,1)S(1)}, u32[]{:S(2)}, u32[]{:S(2)}) collective-permute-start(bf16[3,8,18,1]{3,1,2,0:T(8,128)(2,1)S(1)} %get-tuple-element.71), channel_id=1, source_target_pairs={{1,0},{2,1},{3,2},{0,3},{5,4},{6,5},{7,6},{4,7},{9,8},{10,9},{11,1... | collective-permute-start | bytes 2600 | tf_op jit(solution)/shard_map/ppermute | solution.py:22
  207.9 2.3 %collective-permute-done.7 = bf16[3,8,18,1]{3,1,2,0:T(8,128)(2,1)S(1)} collective-permute-done((bf16[3,8,18,1]{3,1,2,0:T(8,128)(2,1)S(1)}, bf16[3,8,18,1]{3,1,2,0:T(8,128)(2,1)S(1)}, u32[]{:S(2)}, u32[]{:S(2)}) %collective-permute-start.7) | collective-permute-done | bytes 896 | tf_op jit(solution)/shard_map/ppermute | solution.py:22
  210.2 3.3 %collective-permute-done.6 = bf16[3,8,18,1]{3,1,2,0:T(8,128)(2,1)S(1)} collective-permute-done((bf16[3,8,18,1]{3,1,2,0:T(8,128)(2,1)S(1)}, bf16[3,8,18,1]{3,1,2,0:T(8,128)(2,1)S(1)}, u32[]{:S(2)}, u32[]{:S(2)}) %collective-permute-start.6) | collective-permute-done | bytes 896 | tf_op jit(solution)/shard_map/ppermute | solution.py:21
  214.8 1.3 slice.320
  217.1 2.0 maximum_bitcast_fusion.1
  219.6 0.8 add_multiply_fusion
  (208 shorter events, 23.8 us)
Async XLA Ops:
  6.5 55.3 %copy-start = (bf16[1,512,512]{2,1,0:T(8,128)(2,1)S(1)}, bf16[1,512,512]{2,1,0:T(8,128)(2,1)}, u32[]{:S(2)}) copy-start(bf16[1,512,512]{2,1,0:T(8,128)(2,1)} %param.13) | copy-start | bytes 1572868
  8.7 39.7 %copy-start.32 = (f32[16]{0:T(128)}, f32[16]{0:T(128)S(1)}, u32[]{:S(2)}) copy-start(f32[16]{0:T(128)S(1)} %get-tuple-element.95) | copy-start | bytes 196
  9.5 0.6 copy-start.26
  9.6 0.6 copy-start.28
  43.9 17.9 %all-to-all-start = ((bf16[4,2,128]{2,1,0:T(2,128)(2,1)}), bf16[4,2,128]{2,1,0:T(2,128)(2,1)S(1)}, u32[]{:S(2)}, u32[]{:S(2)}) async-start(bf16[4,2,128]{2,1,0:T(2,128)(2,1)} %copy.334), calls=%async_computation | async-start | bytes 4096 | tf_op jit(solution)/shard_map/all_to_all | solution.py:164
  48.5 12.3 %copy-start.24 = (f32[8,2,8]{2,1,0:T(2,128)}, f32[8,2,8]{2,1,0:T(2,128)S(1)}, u32[]{:S(2)}) copy-start(f32[8,2,8]{2,1,0:T(2,128)S(1)} %broadcast_multiply_fusion.3) | copy-start | bytes 1540
  49.4 6.3 %copy-start.2 = (f32[3,8,16,128]{3,2,1,0:T(8,128)S(1)}, f32[3,8,16,128]{3,2,1,0:T(8,128)}, u32[]{:S(2)}) copy-start(f32[3,8,16,128]{3,2,1,0:T(8,128)} %param.12) | copy-start | bytes 589828
  49.4 6.5 %copy-start.1 = (f32[3,8,16,128]{3,2,1,0:T(8,128)S(1)}, f32[3,8,16,128]{3,2,1,0:T(8,128)}, u32[]{:S(2)}) copy-start(f32[3,8,16,128]{3,2,1,0:T(8,128)} %param.11) | copy-start | bytes 589828
  51.6 7.2 %copy-start.10 = (f32[8,16,128]{2,1,0:T(8,128)}, f32[8,16,128]{2,1,0:T(8,128)S(1)}, u32[]{:S(2)}) copy-start(f32[8,16,128]{2,1,0:T(8,128)S(1)} %convolution_bitcast_fusion.6) | copy-start | bytes 196612
  51.6 4.9 %copy-start.22 = (f32[8,8,1,1]{1,0,3,2:T(8,128)S(1)}, f32[8,8,1,1]{1,0,3,2:T(8,128)}, u32[]{:S(2)}) copy-start(f32[8,8,1,1]{1,0,3,2:T(8,128)} %constant.239) | copy-start | bytes 772
  54.3 3.2 %copy-start.23 = (f32[8]{0:T(128)S(1)}, f32[8]{0:T(128)}, u32[]{:S(2)}) copy-start(f32[8]{0:T(128)} %constant.223.clone) | copy-start | bytes 100
  55.2 2.8 %copy-start.3 = (f32[8,8,1]{1,0,2:T(8,128)S(1)}, f32[8,8,1]{1,0,2:T(8,128)}, u32[]{:S(2)}) copy-start(f32[8,8,1]{1,0,2:T(8,128)} %constant.238) | copy-start | bytes 772
  56.0 3.1 %copy-start.4 = (f32[8,16,128]{2,1,0:T(8,128)}, f32[8,16,128]{2,1,0:T(8,128)S(1)}, u32[]{:S(2)}) copy-start(f32[8,16,128]{2,1,0:T(8,128)S(1)} %convolution_bitcast_fusion.5) | copy-start | bytes 196612
  56.5 19.0 %copy-start.6 = (f32[8,16,128]{2,1,0:T(8,128)}, f32[8,16,128]{2,1,0:T(8,128)S(1)}, u32[]{:S(2)}) copy-start(f32[8,16,128]{2,1,0:T(8,128)S(1)} %convolution_bitcast_fusion.9) | copy-start | bytes 196612
  57.0 3.0 %copy-start.31 = (f32[8]{0:T(128)S(1)}, f32[8]{0:T(128)}, u32[]{:S(2)}) copy-start(f32[8]{0:T(128)} %constant.222.clone) | copy-start | bytes 100
  57.0 3.1 %copy-start.30 = (s32[32]{0:T(128)S(1)}, s32[32]{0:T(128)}, u32[]{:S(2)}) copy-start(s32[32]{0:T(128)} %param.14) | copy-start | bytes 388
  57.3 4.0 %copy-start.8 = (f32[8,16,128]{2,1,0:T(8,128)}, f32[8,16,128]{2,1,0:T(8,128)S(1)}, u32[]{:S(2)}) copy-start(f32[8,16,128]{2,1,0:T(8,128)S(1)} %convolution_bitcast_fusion.13) | copy-start | bytes 196612
  57.5 3.8 %copy-start.12 = (f32[8,16,128]{2,1,0:T(8,128)}, f32[8,16,128]{2,1,0:T(8,128)S(1)}, u32[]{:S(2)}) copy-start(f32[8,16,128]{2,1,0:T(8,128)S(1)} %convolution_bitcast_fusion.14) | copy-start | bytes 196612
  58.4 2.7 %copy-start.14 = (f32[8,16,128]{2,0,1:T(8,128)}, f32[8,16,128]{2,0,1:T(8,128)S(1)}, u32[]{:S(2)}) copy-start(f32[8,16,128]{2,0,1:T(8,128)S(1)} %fusion.98) | copy-start | bytes 196612
  59.5 16.0 %copy-start.16 = (f32[8,16,128]{2,0,1:T(8,128)}, f32[8,16,128]{2,0,1:T(8,128)S(1)}, u32[]{:S(2)}) copy-start(f32[8,16,128]{2,0,1:T(8,128)S(1)} %fusion.84) | copy-start | bytes 196612
  60.0 1.8 copy-start.18
  61.8 14.1 %copy-start.20 = (f32[8,16,128]{2,1,0:T(8,128)}, f32[8,16,128]{2,1,0:T(8,128)S(1)}, u32[]{:S(2)}) copy-start(f32[8,16,128]{2,1,0:T(8,128)S(1)} %convolution_bitcast_fusion.10) | copy-start | bytes 196612
  64.6 8.9 %all-to-all-start.1 = ((f32[4,1,256]{2,1,0:T(1,128)}), f32[4,1,256]{2,1,0:T(1,128)S(1)}, u32[]{:S(2)}, u32[]{:S(2)}) async-start(f32[4,1,256]{2,1,0:T(1,128)} %reshape.1012), calls=%async_computation.1 | async-start | bytes 8192 | tf_op jit(solution)/shard_map/all_to_all | solution.py:168
  68.8 33.2 %reduce-scatter.5.cloned.1.call-start = ((), (), s32[]{:S(2)}) async-start(), calls=%async_computation.6 | async-start | bytes 73728 | tf_op jit(solution)/shard_map/reduce_scatter | solution.py:177
  102.8 1.5 collective-permute-start.1
  103.0 4.9 %collective-permute-start = (bf16[3,8,1,128]{3,1,2,0:T(8,128)(2,1)S(1)}, bf16[3,8,1,128]{3,1,2,0:T(8,128)(2,1)S(1)}, u32[]{:S(2)}, u32[]{:S(2)}) collective-permute-start(bf16[3,8,1,128]{3,1,2,0:T(8,128)(2,1)S(1)} %get-tuple-element.76), channel_id=1, source_target_pairs={{0,4},{4,8},{8,12},{12,16},{16,20},{20,24},{24,28},{28,0},{1,5},{5... | collective-permute-start | bytes 18440 | tf_op jit(solution)/shard_map/ppermute | solution.py:21
  108.0 5.0 %collective-permute-start.3 = (bf16[3,8,18,1]{3,1,2,0:T(8,128)(2,1)S(1)}, bf16[3,8,18,1]{3,1,2,0:T(8,128)(2,1)S(1)}, u32[]{:S(2)}, u32[]{:S(2)}) collective-permute-start(bf16[3,8,18,1]{3,1,2,0:T(8,128)(2,1)S(1)} %get-tuple-element.73), channel_id=1, source_target_pairs={{1,0},{2,1},{3,2},{0,3},{5,4},{6,5},{7,6},{4,7},{9,8},{10,9},{11,1... | collective-permute-start | bytes 2600 | tf_op jit(solution)/shard_map/ppermute | solution.py:22
  110.7 5.6 %collective-permute-start.2 = (bf16[3,8,18,1]{3,1,2,0:T(8,128)(2,1)S(1)}, bf16[3,8,18,1]{3,1,2,0:T(8,128)(2,1)S(1)}, u32[]{:S(2)}, u32[]{:S(2)}) collective-permute-start(bf16[3,8,18,1]{3,1,2,0:T(8,128)(2,1)S(1)} %get-tuple-element.72), channel_id=1, source_target_pairs={{0,1},{1,2},{2,3},{3,0},{4,5},{5,6},{6,7},{7,4},{8,9},{9,10},{10,1... | collective-permute-start | bytes 2600 | tf_op jit(solution)/shard_map/ppermute | solution.py:21
  122.0 1.8 copy-start.5
  122.0 1.8 copy-start.7
  122.0 1.8 copy-start.9
  122.0 1.8 copy-start.11
  122.0 1.8 copy-start.13
  122.1 1.8 copy-start.15
  122.1 1.8 copy-start.17
  122.1 1.8 copy-start.19
  122.5 1.4 copy-start.21
  122.5 1.5 copy-start.27
  122.5 1.5 copy-start.29
  122.5 1.5 copy-start.33
  122.5 1.8 copy-start.25
  152.7 7.8 %all-to-all-start.2 = ((bf16[4,2,128]{2,1,0:T(2,128)(2,1)}), bf16[4,2,128]{2,1,0:T(2,128)(2,1)S(1)}, u32[]{:S(2)}, u32[]{:S(2)}) async-start(bf16[4,2,128]{2,1,0:T(2,128)(2,1)} %copy.387), calls=%async_computation.3 | async-start | bytes 4096 | tf_op jit(solution)/shard_map/all_to_all | solution.py:164
  162.7 7.9 %all-to-all-start.3 = ((f32[4,1,256]{2,1,0:T(1,128)}), f32[4,1,256]{2,1,0:T(1,128)S(1)}, u32[]{:S(2)}, u32[]{:S(2)}) async-start(f32[4,1,256]{2,1,0:T(1,128)} %reshape.1014), calls=%async_computation.4 | async-start | bytes 8192 | tf_op jit(solution)/shard_map/all_to_all | solution.py:168
  166.0 33.2 %reduce-scatter.7.cloned.1.call-start = ((), (), s32[]{:S(2)}) async-start(), calls=%async_computation.7 | async-start | bytes 73728 | tf_op jit(solution)/shard_map/reduce_scatter | solution.py:177
  200.0 1.5 collective-permute-start.5
  200.2 4.9 %collective-permute-start.4 = (bf16[3,8,1,128]{3,1,2,0:T(8,128)(2,1)S(1)}, bf16[3,8,1,128]{3,1,2,0:T(8,128)(2,1)S(1)}, u32[]{:S(2)}, u32[]{:S(2)}) collective-permute-start(bf16[3,8,1,128]{3,1,2,0:T(8,128)(2,1)S(1)} %get-tuple-element.74), channel_id=1, source_target_pairs={{0,4},{4,8},{8,12},{12,16},{16,20},{20,24},{24,28},{28,0},{1,5},{5... | collective-permute-start | bytes 18440 | tf_op jit(solution)/shard_map/ppermute | solution.py:21
  205.2 5.0 %collective-permute-start.7 = (bf16[3,8,18,1]{3,1,2,0:T(8,128)(2,1)S(1)}, bf16[3,8,18,1]{3,1,2,0:T(8,128)(2,1)S(1)}, u32[]{:S(2)}, u32[]{:S(2)}) collective-permute-start(bf16[3,8,18,1]{3,1,2,0:T(8,128)(2,1)S(1)} %get-tuple-element.71), channel_id=1, source_target_pairs={{1,0},{2,1},{3,2},{0,3},{5,4},{6,5},{7,6},{4,7},{9,8},{10,9},{11,1... | collective-permute-start | bytes 2600 | tf_op jit(solution)/shard_map/ppermute | solution.py:22
  207.9 5.6 %collective-permute-start.6 = (bf16[3,8,18,1]{3,1,2,0:T(8,128)(2,1)S(1)}, bf16[3,8,18,1]{3,1,2,0:T(8,128)(2,1)S(1)}, u32[]{:S(2)}, u32[]{:S(2)}) collective-permute-start(bf16[3,8,18,1]{3,1,2,0:T(8,128)(2,1)S(1)} %get-tuple-element.70), channel_id=1, source_target_pairs={{0,1},{1,2},{2,3},{3,0},{4,5},{5,6},{6,7},{7,4},{8,9},{9,10},{10,1... | collective-permute-start | bytes 2600 | tf_op jit(solution)/shard_map/ppermute | solution.py:21
Sparse Core Ops, SparseCore 0:
  75.7 26.3 reduce-scatter.4
  172.8 26.3 reduce-scatter.6
where the time goes:
time: 228 us; the launch traced here: 227 us
  waiting for transfers between devices  84.8 us (37%)
  blocking collectives  56.3 us (25%)
  starting transfers between devices  21 us (9%)
  local copies, waits for them, and re-layouts  17.1 us (8%)
  matrix products  16.9 us (7%)
  other arithmetic  15.9 us (7%)
  between operations  15.3 us (7%)
    unnamed x2, blocking collectives  56.3 us
    reduce_scatter x2, waiting for transfers between devices, surface_flux(): lax.psum_scatter(jnp.dot(table, flat_matched, precision=highest), 'tile',...  52.2 us
    ppermute x4, waiting for transfers between devices, padded_2(): before = lax.ppermute(last, axis, up)  13.6 us
    dot_general x30, matrix products, apply_along(): return jnp.einsum(formula, blocks, matrix, precision=highest).reshape(shape)  9.26 us
    all_to_all x2, waiting for transfers between devices, surface_flux(): lax.all_to_all(mapped, 'deg', split_axis=2, concat_axis=0, tiled=True)  8.98 us
    all_to_all x2, starting transfers between devices, surface_flux(): lax.all_to_all(mapped, 'deg', split_axis=2, concat_axis=0, tiled=True)  7.44 us
    all_to_all x2, starting transfers between devices, surface_flux(): lax.all_to_all(coeff.astype(jnp.bfloat16), 'deg', split_axis=0, concat_ax...  6.94 us
    unnamed x81, local copies, waits for them, and re-layouts  6.64 us
  transfers between devices with their start and end apart: 14, of which 13 were waited for; matrix products, arithmetic and copies ran while one was open for 7% of the time, Pallas kernels for 0%

commit v1 on v0

--- a/solution.py
+++ b/solution.py
@@ -9,6 +9,18 @@
 time_step = 0.01
 highest = lax.Precision.HIGHEST
 gll_interior = [0.2092992179024789, 0.5917001814331423, 0.8717401485096066]
+
+
+def cut_along(shard, dim, size):
+    shape = shard.shape
+    blocks = shard.reshape(*shape[:dim], size, shape[dim] // size, *shape[dim + 1 :])
+    return jnp.moveaxis(blocks, dim, 0)
+
+
+def in_order(blocks, dim):
+    blocks = jnp.moveaxis(blocks, 0, dim)
+    shape = blocks.shape
+    return blocks.reshape(*shape[:dim], shape[dim] * shape[dim + 1], *shape[dim + 2 :])
 
 
 def padded_2(value, sides, width):
@@ -165,7 +177,16 @@
             coeff.astype(jnp.bfloat16), "deg", split_axis=0, concat_axis=2, tiled=True
         )
         mapped = jnp.einsum("kpq,kcq->kcp", match_ops, owned, preferred_element_type=jnp.float32)
-        matched = lax.all_to_all(mapped, "deg", split_axis=2, concat_axis=0, tiled=True)
+        count_2, mine = (lax.axis_size("deg"), lax.axis_index("deg"))
+        tiles_2 = cut_along(mapped, 2, count_2)
+        finished = [tiles_2[mine]]
+        for lap in range(1, count_2):
+            sent = tiles_2[(mine + lap) % count_2]
+            finished.append(
+                lax.ppermute(sent, "deg", [(i_2, (i_2 + lap) % count_2) for i_2 in range(count_2)])
+            )
+        tiles_2 = jnp.stack(finished)[(mine - jnp.arange(count_2)) % count_2]
+        matched = in_order(tiles_2, 0)
         my_waves = lax.dynamic_slice_in_dim(wave_of_slot, tile_index * per_tile, per_tile)
         flat_matched = matched.reshape(per_tile * 2, nb_dev)
         angle = phases(

time: 228 us -> 221 us (0.969)
  other arithmetic: 15.9 us -> 12.3 us
    all_to_all x2 -> x0, waiting for transfers between devices: 8.98 us -> none  [surface_flux(): lax.all_to_all(mapped, 'deg', split_axis=2, concat_axis=0, tiled=True)]
    ppermute x0 -> x6, waiting for transfers between devices: none -> 7.52 us  [surface_flux(): lax.ppermute(sent, 'deg', [(i_2, (i_2 + lap) % count_2) for i_2 in range(...]
    all_to_all x2 -> x0, starting transfers between devices: 7.44 us -> none  [surface_flux(): lax.all_to_all(mapped, 'deg', split_axis=2, concat_axis=0, tiled=True)]
    ppermute x0 -> x6, starting transfers between devices: none -> 6.83 us  [surface_flux(): lax.ppermute(sent, 'deg', [(i_2, (i_2 + lap) % count_2) for i_2 in range(...]
    unnamed x81 -> x80, local copies, waits for them, and re-layouts: 6.64 us -> 3.8 us
    unnamed x2 -> x0, other arithmetic: 2.44 us -> none
  transfers between devices with their start and end apart: 14 -> 18, of which waited for: 13 -> 17; matrix products, arithmetic and copies ran while one was open for 7% -> 7% of each run, Pallas kernels for 0% -> 0%
where the time goes in v1:
time: 221 us; the launch traced here: 220 us
  waiting for transfers between devices  84.1 us (38%)
  blocking collectives  56.3 us (25%)
  starting transfers between devices  20.3 us (9%)
  matrix products  16.8 us (8%)
  between operations  15.3 us (7%)
  local copies, waits for them, and re-layouts  15.2 us (7%)
  other arithmetic  12.3 us (6%)
    unnamed x2, blocking collectives  56.3 us
    reduce_scatter x2, waiting for transfers between devices, surface_flux(): lax.psum_scatter(jnp.dot(table, flat_matched, precision=highest), 'tile',...  53.1 us
    ppermute x4, waiting for transfers between devices, padded_2(): before = lax.ppermute(last, axis, up)  13.6 us
    dot_general x30, matrix products, apply_along(): return jnp.einsum(formula, blocks, matrix, precision=highest).reshape(shape)  9.27 us
    ppermute x6, waiting for transfers between devices, surface_flux(): lax.ppermute(sent, 'deg', [(i_2, (i_2 + lap) % count_2) for i_2 in range(...  7.52 us
    all_to_all x2, starting transfers between devices, surface_flux(): lax.all_to_all(coeff.astype(jnp.bfloat16), 'deg', split_axis=0, concat_ax...  6.94 us
    ppermute x6, starting transfers between devices, surface_flux(): lax.ppermute(sent, 'deg', [(i_2, (i_2 + lap) % count_2) for i_2 in range(...  6.83 us
    ppermute x4, waiting for transfers between devices, padded_2(): after = lax.ppermute(first, axis, down)  6.39 us
  transfers between devices with their start and end apart: 18, of which 17 were waited for; matrix products, arithmetic and copies ran while one was open for 7% of the time, Pallas kernels for 0%

profile of v1, /device:TPU:0, one launch (start us, length us, event | category | flops | bytes accessed | tf_op | source)
XLA Modules:
  0.0 220.3 jit_solution(5791490967847780379)
XLA Ops:
  6.5 0.7 tile.8
  7.3 0.7 tile.11
  8.1 0.7 convert_element_type.71
  8.8 0.8 fusion.126
  10.2 1.0 fusion.112
  11.2 30.3 %all-reduce = bf16[32,2,128]{2,0,1:T(8,128)(2,1)S(1)} all-reduce(f32[32,2,128]{2,0,1:T(8,128)S(1)} %fusion.112), channel_id=2, replica_groups=mesh['tile'=8,'deg'=4] {'tile'}, use_global_device_ids=true, to_apply=%region_0.1.clone | all-reduce | flops 8192 | bytes 49152
  41.5 1.2 dynamic-slice.56
  43.9 3.7 %all-to-all-start = ((bf16[4,2,128]{2,1,0:T(2,128)(2,1)}), bf16[4,2,128]{2,1,0:T(2,128)(2,1)S(1)}, u32[]{:S(2)}, u32[]{:S(2)}) async-start(bf16[4,2,128]{2,1,0:T(2,128)(2,1)} %copy.328), calls=%async_computation | async-start | bytes 4096 | tf_op jit(solution)/shard_map/all_to_all | solution.py:176
  47.7 0.8 broadcast_multiply_fusion.3
  48.5 0.9 slice_bitcast_fusion.6
  49.4 1.1 fusion.47
  50.5 1.0 convolution_bitcast_fusion.6
  51.6 0.9 fusion.177
  52.6 0.7 broadcast_multiply_fusion.5
  53.3 1.0 fusion.50
  54.4 0.8 broadcast_multiply_fusion
  62.1 2.9 %collective-permute-start.2 = (f32[1,2,128]{2,1,0:T(2,128)S(1)}, f32[1,2,128]{2,1,0:T(2,128)S(1)}, u32[]{:S(2)}, u32[]{:S(2)}) collective-permute-start(f32[1,2,128]{2,1,0:T(2,128)S(1)} %get-tuple-element.95), channel_id=1, source_target_pairs={{0,3},{1,0},{2,1},{3,2},{4,7},{5,4},{6,5},{7,6},{8,11},{9,8},{10,9... | collective-permute-start | bytes 3080 | tf_op jit(solution)/shard_map/ppermute | solution.py:186
  66.4 2.3 %collective-permute-done.1 = f32[1,2,128]{2,1,0:T(2,128)S(1)} collective-permute-done((f32[1,2,128]{2,1,0:T(2,128)S(1)}, f32[1,2,128]{2,1,0:T(2,128)S(1)}, u32[]{:S(2)}, u32[]{:S(2)}) %collective-permute-start.1) | collective-permute-done | bytes 1056 | tf_op jit(solution)/shard_map/ppermute | solution.py:186
  68.6 1.5 collective-permute-done
  70.7 0.9 fusion.180
  72.2 26.8 %reduce-scatter.5.cloned.1.call-done = f32[16,128]{1,0:T(8,128)} async-done(((f32[128,128]{1,0:T(8,128)}), f32[16,128]{1,0:T(8,128)}) %reduce-scatter.5.cloned.1.call-update) | async-done | bytes 8208 | tf_op jit(solution)/shard_map/reduce_scatter | solution.py:198
  99.0 0.8 fusion.119
  100.5 0.9 collective-permute-done.4
  101.3 3.5 %collective-permute-done.3 = bf16[3,8,1,128]{3,1,2,0:T(8,128)(2,1)S(1)} collective-permute-done((bf16[3,8,1,128]{3,1,2,0:T(8,128)(2,1)S(1)}, bf16[3,8,1,128]{3,1,2,0:T(8,128)(2,1)S(1)}, u32[]{:S(2)}, u32[]{:S(2)}) %collective-permute-start.3) | collective-permute-done | bytes 6176 | tf_op jit(solution)/shard_map/ppermute | solution.py:33
  105.0 2.7 %collective-permute-start.6 = (bf16[3,8,18,1]{3,1,2,0:T(8,128)(2,1)S(1)}, bf16[3,8,18,1]{3,1,2,0:T(8,128)(2,1)S(1)}, u32[]{:S(2)}, u32[]{:S(2)}) collective-permute-start(bf16[3,8,18,1]{3,1,2,0:T(8,128)(2,1)S(1)} %get-tuple-element.73), channel_id=1, source_target_pairs={{1,0},{2,1},{3,2},{0,3},{5,4},{6,5},{7,6},{4,7},{9,8},{10,9},{11,1... | collective-permute-start | bytes 2600 | tf_op jit(solution)/shard_map/ppermute | solution.py:34
  107.8 2.2 %collective-permute-done.6 = bf16[3,8,18,1]{3,1,2,0:T(8,128)(2,1)S(1)} collective-permute-done((bf16[3,8,18,1]{3,1,2,0:T(8,128)(2,1)S(1)}, bf16[3,8,18,1]{3,1,2,0:T(8,128)(2,1)S(1)}, u32[]{:S(2)}, u32[]{:S(2)}) %collective-permute-start.6) | collective-permute-done | bytes 896 | tf_op jit(solution)/shard_map/ppermute | solution.py:34
  110.0 3.3 %collective-permute-done.5 = bf16[3,8,18,1]{3,1,2,0:T(8,128)(2,1)S(1)} collective-permute-done((bf16[3,8,18,1]{3,1,2,0:T(8,128)(2,1)S(1)}, bf16[3,8,18,1]{3,1,2,0:T(8,128)(2,1)S(1)}, u32[]{:S(2)}, u32[]{:S(2)}) %collective-permute-start.5) | collective-permute-done | bytes 896 | tf_op jit(solution)/shard_map/ppermute | solution.py:33
  114.6 1.3 slice.301
  116.9 2.0 maximum_bitcast_fusion
  123.1 26.0 %all-reduce.1 = bf16[32,2,128]{2,0,1:T(8,128)(2,1)S(1)} all-reduce(f32[32,2,128]{2,0,1:T(8,128)S(1)} %fusion.111), channel_id=4, replica_groups=mesh['tile'=8,'deg'=4] {'tile'}, use_global_device_ids=true, to_apply=%region_2.3.clone | all-reduce | flops 8192 | bytes 49152
  149.0 0.6 copy.379
  149.6 3.2 %all-to-all-start.1 = ((bf16[4,2,128]{2,1,0:T(2,128)(2,1)}), bf16[4,2,128]{2,1,0:T(2,128)(2,1)S(1)}, u32[]{:S(2)}, u32[]{:S(2)}) async-start(bf16[4,2,128]{2,1,0:T(2,128)(2,1)} %copy.379), calls=%async_computation.2 | async-start | bytes 4096 | tf_op jit(solution)/shard_map/all_to_all | solution.py:176
  153.9 3.4 %all-to-all-done.1 = bf16[4,2,128]{2,1,0:T(2,128)(2,1)S(1)} async-done(((bf16[4,2,128]{2,1,0:T(2,128)(2,1)}), bf16[4,2,128]{2,1,0:T(2,128)(2,1)S(1)}, u32[]{:S(2)}, u32[]{:S(2)}) %all-to-all-start.1) | async-done | bytes 2080 | tf_op jit(solution)/shard_map/all_to_all | solution.py:176
  157.6 0.7 collective-permute-start.9
  158.3 1.5 collective-permute-start.8
  160.6 0.7 collective-permute-done.9
  161.9 2.4 %collective-permute-done.7 = f32[1,2,128]{2,1,0:T(2,128)S(1)} collective-permute-done((f32[1,2,128]{2,1,0:T(2,128)S(1)}, f32[1,2,128]{2,1,0:T(2,128)S(1)}, u32[]{:S(2)}, u32[]{:S(2)}) %collective-permute-start.7) | collective-permute-done | bytes 1056 | tf_op jit(solution)/shard_map/ppermute | solution.py:186
  164.9 0.9 fusion.181
  166.0 26.3 %reduce-scatter.7.cloned.1.call-done = f32[16,128]{1,0:T(8,128)} async-done(((f32[128,128]{1,0:T(8,128)}), f32[16,128]{1,0:T(8,128)}) %reduce-scatter.7.cloned.1.call-update) | async-done | bytes 8208 | tf_op jit(solution)/shard_map/reduce_scatter | solution.py:198
  192.3 0.8 negate_multiply_fusion
  193.8 0.9 collective-permute-done.11
  194.7 3.5 %collective-permute-done.10 = bf16[3,8,1,128]{3,1,2,0:T(8,128)(2,1)S(1)} collective-permute-done((bf16[3,8,1,128]{3,1,2,0:T(8,128)(2,1)S(1)}, bf16[3,8,1,128]{3,1,2,0:T(8,128)(2,1)S(1)}, u32[]{:S(2)}, u32[]{:S(2)}) %collective-permute-start.10) | collective-permute-done | bytes 6176 | tf_op jit(solution)/shard_map/ppermute | solution.py:33
  198.3 2.7 %collective-permute-start.13 = (bf16[3,8,18,1]{3,1,2,0:T(8,128)(2,1)S(1)}, bf16[3,8,18,1]{3,1,2,0:T(8,128)(2,1)S(1)}, u32[]{:S(2)}, u32[]{:S(2)}) collective-permute-start(bf16[3,8,18,1]{3,1,2,0:T(8,128)(2,1)S(1)} %get-tuple-element.71), channel_id=1, source_target_pairs={{1,0},{2,1},{3,2},{0,3},{5,4},{6,5},{7,6},{4,7},{9,8},{10,9},{11,1... | collective-permute-start | bytes 2600 | tf_op jit(solution)/shard_map/ppermute | solution.py:34
  201.0 2.3 %collective-permute-done.13 = bf16[3,8,18,1]{3,1,2,0:T(8,128)(2,1)S(1)} collective-permute-done((bf16[3,8,18,1]{3,1,2,0:T(8,128)(2,1)S(1)}, bf16[3,8,18,1]{3,1,2,0:T(8,128)(2,1)S(1)}, u32[]{:S(2)}, u32[]{:S(2)}) %collective-permute-start.13) | collective-permute-done | bytes 896 | tf_op jit(solution)/shard_map/ppermute | solution.py:34
  203.3 3.3 %collective-permute-done.12 = bf16[3,8,18,1]{3,1,2,0:T(8,128)(2,1)S(1)} collective-permute-done((bf16[3,8,18,1]{3,1,2,0:T(8,128)(2,1)S(1)}, bf16[3,8,18,1]{3,1,2,0:T(8,128)(2,1)S(1)}, u32[]{:S(2)}, u32[]{:S(2)}) %collective-permute-start.12) | collective-permute-done | bytes 896 | tf_op jit(solution)/shard_map/ppermute | solution.py:33
  208.0 1.3 slice.324
  210.3 2.0 maximum_bitcast_fusion.1
  212.7 0.8 add_multiply_fusion
  (217 shorter events, 24.0 us)
Async XLA Ops:
  6.5 55.3 %copy-start = (bf16[1,512,512]{2,1,0:T(8,128)(2,1)S(1)}, bf16[1,512,512]{2,1,0:T(8,128)(2,1)}, u32[]{:S(2)}) copy-start(bf16[1,512,512]{2,1,0:T(8,128)(2,1)} %param.13) | copy-start | bytes 1572868
  7.3 91.7 %copy-start.30 = (f32[16]{0:T(128)}, f32[16]{0:T(128)S(1)}, u32[]{:S(2)}) copy-start(f32[16]{0:T(128)S(1)} %mul.669) | copy-start | bytes 196
  8.8 39.7 %copy-start.34 = (f32[16]{0:T(128)}, f32[16]{0:T(128)S(1)}, u32[]{:S(2)}) copy-start(f32[16]{0:T(128)S(1)} %get-tuple-element.103) | copy-start | bytes 196
  43.9 17.9 %all-to-all-start = ((bf16[4,2,128]{2,1,0:T(2,128)(2,1)}), bf16[4,2,128]{2,1,0:T(2,128)(2,1)S(1)}, u32[]{:S(2)}, u32[]{:S(2)}) async-start(bf16[4,2,128]{2,1,0:T(2,128)(2,1)} %copy.328), calls=%async_computation | async-start | bytes 4096 | tf_op jit(solution)/shard_map/all_to_all | solution.py:176
  47.7 51.4 %reduce-scatter.5.cloned.1.call-start = ((), (), s32[]{:S(2)}) async-start(), calls=%async_computation.4 | async-start | bytes 73728 | tf_op jit(solution)/shard_map/reduce_scatter | solution.py:198
  48.5 12.6 %copy-start.24 = (f32[8,2,8]{2,1,0:T(2,128)}, f32[8,2,8]{2,1,0:T(2,128)S(1)}, u32[]{:S(2)}) copy-start(f32[8,2,8]{2,1,0:T(2,128)S(1)} %broadcast_multiply_fusion.3) | copy-start | bytes 1540
  49.4 6.3 %copy-start.2 = (f32[3,8,16,128]{3,2,1,0:T(8,128)S(1)}, f32[3,8,16,128]{3,2,1,0:T(8,128)}, u32[]{:S(2)}) copy-start(f32[3,8,16,128]{3,2,1,0:T(8,128)} %param.12) | copy-start | bytes 589828
  49.4 6.5 %copy-start.1 = (f32[3,8,16,128]{3,2,1,0:T(8,128)S(1)}, f32[3,8,16,128]{3,2,1,0:T(8,128)}, u32[]{:S(2)}) copy-start(f32[3,8,16,128]{3,2,1,0:T(8,128)} %param.11) | copy-start | bytes 589828
  51.6 7.4 %copy-start.10 = (f32[8,16,128]{2,1,0:T(8,128)}, f32[8,16,128]{2,1,0:T(8,128)S(1)}, u32[]{:S(2)}) copy-start(f32[8,16,128]{2,1,0:T(8,128)S(1)} %convolution_bitcast_fusion.6) | copy-start | bytes 196612
  51.6 4.9 %copy-start.22 = (f32[8,8,1,1]{1,0,3,2:T(8,128)S(1)}, f32[8,8,1,1]{1,0,3,2:T(8,128)}, u32[]{:S(2)}) copy-start(f32[8,8,1,1]{1,0,3,2:T(8,128)} %constant.276) | copy-start | bytes 772
  54.3 3.4 %copy-start.23 = (f32[8]{0:T(128)S(1)}, f32[8]{0:T(128)}, u32[]{:S(2)}) copy-start(f32[8]{0:T(128)} %constant.260.clone) | copy-start | bytes 100
  55.2 3.0 %copy-start.3 = (f32[8,8,1]{1,0,2:T(8,128)S(1)}, f32[8,8,1]{1,0,2:T(8,128)}, u32[]{:S(2)}) copy-start(f32[8,8,1]{1,0,2:T(8,128)} %constant.275) | copy-start | bytes 772
  56.0 3.3 %copy-start.4 = (f32[8,16,128]{2,1,0:T(8,128)}, f32[8,16,128]{2,1,0:T(8,128)S(1)}, u32[]{:S(2)}) copy-start(f32[8,16,128]{2,1,0:T(8,128)S(1)} %convolution_bitcast_fusion.5) | copy-start | bytes 196612
  56.5 15.1 %copy-start.6 = (f32[8,16,128]{2,1,0:T(8,128)}, f32[8,16,128]{2,1,0:T(8,128)S(1)}, u32[]{:S(2)}) copy-start(f32[8,16,128]{2,1,0:T(8,128)S(1)} %convolution_bitcast_fusion.9) | copy-start | bytes 196612
  56.7 14.9 %copy-start.12 = (f32[8,16,128]{2,1,0:T(8,128)}, f32[8,16,128]{2,1,0:T(8,128)S(1)}, u32[]{:S(2)}) copy-start(f32[8,16,128]{2,1,0:T(8,128)S(1)} %convolution_bitcast_fusion.10) | copy-start | bytes 196612
  57.2 3.0 %copy-start.33 = (f32[8]{0:T(128)S(1)}, f32[8]{0:T(128)}, u32[]{:S(2)}) copy-start(f32[8]{0:T(128)} %constant.259.clone) | copy-start | bytes 100
  57.2 3.1 %copy-start.32 = (s32[32]{0:T(128)S(1)}, s32[32]{0:T(128)}, u32[]{:S(2)}) copy-start(s32[32]{0:T(128)} %param.14) | copy-start | bytes 388
  57.5 4.0 %copy-start.8 = (f32[8,16,128]{2,1,0:T(8,128)}, f32[8,16,128]{2,1,0:T(8,128)S(1)}, u32[]{:S(2)}) copy-start(f32[8,16,128]{2,1,0:T(8,128)S(1)} %convolution_bitcast_fusion.13) | copy-start | bytes 196612
  57.7 3.8 %copy-start.14 = (f32[8,16,128]{2,1,0:T(8,128)}, f32[8,16,128]{2,1,0:T(8,128)S(1)}, u32[]{:S(2)}) copy-start(f32[8,16,128]{2,1,0:T(8,128)S(1)} %convolution_bitcast_fusion.14) | copy-start | bytes 196612
  58.6 2.7 %copy-start.16 = (f32[8,16,128]{2,0,1:T(8,128)}, f32[8,16,128]{2,0,1:T(8,128)S(1)}, u32[]{:S(2)}) copy-start(f32[8,16,128]{2,0,1:T(8,128)S(1)} %fusion.94) | copy-start | bytes 196612
  59.8 11.9 %copy-start.18 = (f32[8,16,128]{2,0,1:T(8,128)}, f32[8,16,128]{2,0,1:T(8,128)S(1)}, u32[]{:S(2)}) copy-start(f32[8,16,128]{2,0,1:T(8,128)S(1)} %fusion.80) | copy-start | bytes 196612
  60.3 11.7 %copy-start.20 = (f32[8,16,128]{2,0,1:T(8,128)}, f32[8,16,128]{2,0,1:T(8,128)S(1)}, u32[]{:S(2)}) copy-start(f32[8,16,128]{2,0,1:T(8,128)S(1)} %fusion.86) | copy-start | bytes 196612
  62.1 4.2 %collective-permute-start.2 = (f32[1,2,128]{2,1,0:T(2,128)S(1)}, f32[1,2,128]{2,1,0:T(2,128)S(1)}, u32[]{:S(2)}, u32[]{:S(2)}) collective-permute-start(f32[1,2,128]{2,1,0:T(2,128)S(1)} %get-tuple-element.95), channel_id=1, source_target_pairs={{0,3},{1,0},{2,1},{3,2},{4,7},{5,4},{6,5},{7,6},{8,11},{9,8},{10,9... | collective-permute-start | bytes 3080 | tf_op jit(solution)/shard_map/ppermute | solution.py:186
  65.1 3.6 %collective-permute-start.1 = (f32[1,2,128]{2,1,0:T(2,128)S(1)}, f32[1,2,128]{2,1,0:T(2,128)S(1)}, u32[]{:S(2)}, u32[]{:S(2)}) collective-permute-start(f32[1,2,128]{2,1,0:T(2,128)S(1)} %get-tuple-element.96), channel_id=1, source_target_pairs={{0,2},{1,3},{2,0},{3,1},{4,6},{5,7},{6,4},{7,5},{8,10},{9,11},{10,... | collective-permute-start | bytes 3080 | tf_op jit(solution)/shard_map/ppermute | solution.py:186
  65.6 4.5 %collective-permute-start = (f32[1,2,128]{2,1,0:T(2,128)S(1)}, f32[1,2,128]{2,1,0:T(2,128)S(1)}, u32[]{:S(2)}, u32[]{:S(2)}) collective-permute-start(f32[1,2,128]{2,1,0:T(2,128)S(1)} %get-tuple-element.97), channel_id=1, source_target_pairs={{0,1},{1,2},{2,3},{3,0},{4,5},{5,6},{6,7},{7,4},{8,9},{9,10},{10,1... | collective-permute-start | bytes 3080 | tf_op jit(solution)/shard_map/ppermute | solution.py:186
  99.8 1.5 collective-permute-start.4
  100.0 4.9 %collective-permute-start.3 = (bf16[3,8,1,128]{3,1,2,0:T(8,128)(2,1)S(1)}, bf16[3,8,1,128]{3,1,2,0:T(8,128)(2,1)S(1)}, u32[]{:S(2)}, u32[]{:S(2)}) collective-permute-start(bf16[3,8,1,128]{3,1,2,0:T(8,128)(2,1)S(1)} %get-tuple-element.76), channel_id=1, source_target_pairs={{0,4},{4,8},{8,12},{12,16},{16,20},{20,24},{24,28},{28,0},{1,5},{5... | collective-permute-start | bytes 18440 | tf_op jit(solution)/shard_map/ppermute | solution.py:33
  105.0 5.0 %collective-permute-start.6 = (bf16[3,8,18,1]{3,1,2,0:T(8,128)(2,1)S(1)}, bf16[3,8,18,1]{3,1,2,0:T(8,128)(2,1)S(1)}, u32[]{:S(2)}, u32[]{:S(2)}) collective-permute-start(bf16[3,8,18,1]{3,1,2,0:T(8,128)(2,1)S(1)} %get-tuple-element.73), channel_id=1, source_target_pairs={{1,0},{2,1},{3,2},{0,3},{5,4},{6,5},{7,6},{4,7},{9,8},{10,9},{11,1... | collective-permute-start | bytes 2600 | tf_op jit(solution)/shard_map/ppermute | solution.py:34
  107.7 5.6 %collective-permute-start.5 = (bf16[3,8,18,1]{3,1,2,0:T(8,128)(2,1)S(1)}, bf16[3,8,18,1]{3,1,2,0:T(8,128)(2,1)S(1)}, u32[]{:S(2)}, u32[]{:S(2)}) collective-permute-start(bf16[3,8,18,1]{3,1,2,0:T(8,128)(2,1)S(1)} %get-tuple-element.72), channel_id=1, source_target_pairs={{0,1},{1,2},{2,3},{3,0},{4,5},{5,6},{6,7},{7,4},{8,9},{9,10},{10,1... | collective-permute-start | bytes 2600 | tf_op jit(solution)/shard_map/ppermute | solution.py:33
  119.0 1.8 copy-start.5
  119.0 1.8 copy-start.7
  119.0 1.8 copy-start.9
  119.0 1.8 copy-start.11
  119.0 1.8 copy-start.13
  119.0 1.8 copy-start.15
  119.0 1.8 copy-start.17
  119.0 1.8 copy-start.19
  119.5 1.8 copy-start.25
  149.6 7.8 %all-to-all-start.1 = ((bf16[4,2,128]{2,1,0:T(2,128)(2,1)}), bf16[4,2,128]{2,1,0:T(2,128)(2,1)S(1)}, u32[]{:S(2)}, u32[]{:S(2)}) async-start(bf16[4,2,128]{2,1,0:T(2,128)(2,1)} %copy.379), calls=%async_computation.2 | async-start | bytes 4096 | tf_op jit(solution)/shard_map/all_to_all | solution.py:176
  152.9 39.5 %reduce-scatter.7.cloned.1.call-start = ((), (), s32[]{:S(2)}) async-start(), calls=%async_computation.5 | async-start | bytes 73728 | tf_op jit(solution)/shard_map/reduce_scatter | solution.py:198
  152.9 39.4 %copy-start.31 = (f32[16]{0:T(128)S(1)}, f32[16]{0:T(128)}, u32[]{:S(2)}) copy-start(f32[16]{0:T(128)} %copy-done.30) | copy-start | bytes 196
  157.6 3.7 %collective-permute-start.9 = (f32[1,2,128]{2,1,0:T(2,128)S(1)}, f32[1,2,128]{2,1,0:T(2,128)S(1)}, u32[]{:S(2)}, u32[]{:S(2)}) collective-permute-start(f32[1,2,128]{2,1,0:T(2,128)S(1)} %get-tuple-element.91), channel_id=1, source_target_pairs={{0,3},{1,0},{2,1},{3,2},{4,7},{5,4},{6,5},{7,6},{8,11},{9,8},{10,9... | collective-permute-start | bytes 3080 | tf_op jit(solution)/shard_map/ppermute | solution.py:186
  158.3 3.6 %collective-permute-start.8 = (f32[1,2,128]{2,1,0:T(2,128)S(1)}, f32[1,2,128]{2,1,0:T(2,128)S(1)}, u32[]{:S(2)}, u32[]{:S(2)}) collective-permute-start(f32[1,2,128]{2,1,0:T(2,128)S(1)} %get-tuple-element.92), channel_id=1, source_target_pairs={{0,2},{1,3},{2,0},{3,1},{4,6},{5,7},{6,4},{7,5},{8,10},{9,11},{10,... | collective-permute-start | bytes 3080 | tf_op jit(solution)/shard_map/ppermute | solution.py:186
  159.8 4.5 %collective-permute-start.7 = (f32[1,2,128]{2,1,0:T(2,128)S(1)}, f32[1,2,128]{2,1,0:T(2,128)S(1)}, u32[]{:S(2)}, u32[]{:S(2)}) collective-permute-start(f32[1,2,128]{2,1,0:T(2,128)S(1)} %get-tuple-element.93), channel_id=1, source_target_pairs={{0,1},{1,2},{2,3},{3,0},{4,5},{5,6},{6,7},{7,4},{8,9},{9,10},{10,1... | collective-permute-start | bytes 3080 | tf_op jit(solution)/shard_map/ppermute | solution.py:186
  193.2 1.5 collective-permute-start.11
  193.4 4.9 %collective-permute-start.10 = (bf16[3,8,1,128]{3,1,2,0:T(8,128)(2,1)S(1)}, bf16[3,8,1,128]{3,1,2,0:T(8,128)(2,1)S(1)}, u32[]{:S(2)}, u32[]{:S(2)}) collective-permute-start(bf16[3,8,1,128]{3,1,2,0:T(8,128)(2,1)S(1)} %get-tuple-element.74), channel_id=1, source_target_pairs={{0,4},{4,8},{8,12},{12,16},{16,20},{20,24},{24,28},{28,0},{1,5},{5... | collective-permute-start | bytes 18440 | tf_op jit(solution)/shard_map/ppermute | solution.py:33
  198.3 5.0 %collective-permute-start.13 = (bf16[3,8,18,1]{3,1,2,0:T(8,128)(2,1)S(1)}, bf16[3,8,18,1]{3,1,2,0:T(8,128)(2,1)S(1)}, u32[]{:S(2)}, u32[]{:S(2)}) collective-permute-start(bf16[3,8,18,1]{3,1,2,0:T(8,128)(2,1)S(1)} %get-tuple-element.71), channel_id=1, source_target_pairs={{1,0},{2,1},{3,2},{0,3},{5,4},{6,5},{7,6},{4,7},{9,8},{10,9},{11,1... | collective-permute-start | bytes 2600 | tf_op jit(solution)/shard_map/ppermute | solution.py:34
  201.0 5.6 %collective-permute-start.12 = (bf16[3,8,18,1]{3,1,2,0:T(8,128)(2,1)S(1)}, bf16[3,8,18,1]{3,1,2,0:T(8,128)(2,1)S(1)}, u32[]{:S(2)}, u32[]{:S(2)}) collective-permute-start(bf16[3,8,18,1]{3,1,2,0:T(8,128)(2,1)S(1)} %get-tuple-element.70), channel_id=1, source_target_pairs={{0,1},{1,2},{2,3},{3,0},{4,5},{5,6},{6,7},{7,4},{8,9},{9,10},{10,1... | collective-permute-start | bytes 2600 | tf_op jit(solution)/shard_map/ppermute | solution.py:33
  (6 other events, 7.0 us)
Sparse Core Ops, SparseCore 0:
  71.7 27.2 reduce-scatter.4
  165.9 26.3 reduce-scatter.6
